TPU v7x, 128 devices: a whole 4x4x4 slice. The times are simulated.
128 devices in a mesh: row: 4 (over x), col: 32 (over z, y, core).
Axes of the slice: x: 4, y: 4, z: 4, core: 2. Of those that a mesh axis runs over, the one named last changes fastest.
Arguments:
- child_factors: bfloat16 [2, 2048, 8192], P(None, 'col', 'row'), may hold values from -0.0625 to 0.0625
- child_tiles: int32 [2, 16], replicated, may hold values from 0 to 63, as said below
- root_diag: float32 [8192], P('col'), may hold values from 0.5 to 4
Outputs:
- front_out: float32 [8192, 8192], P('row', 'col')
Inputs may be any that keep to these rules, and one draw needn't show every extreme that they name: `child_tiles`: each row lists 2048 / 128 distinct root tiles in increasing order; the first child's list holds tile 0 and the second child's holds the last tile. For every r below 4, exactly 2048 / (128 * 4) tiles t of each row have ((t * 128) // 256) % 4 == r.
All inputs are finite; a program needn't handle non-finite values.
Results may differ from a plain program's by a relative error of at most 0.0003.
Values may be sent and summed in bfloat16 or wider, within the bound.
No kernel may reach another device: no remote copies, remote signals or barrier semaphores. Data moves between devices by JAX's collectives and lax.ppermute only.
A program may use at most 128 MiB of HBM per device.

v0:
```python
import jax
import jax.numpy as jnp
from jax import lax
from jax.sharding import PartitionSpec as P

TILE = 128
NPAN = 1


def pick_tiles(tiles4, index):
    return jnp.take_along_axis(tiles4, index[:, :, None, None], axis=1)


def shards(child_factors, child_tiles, root_diag):
    highest = lax.Precision.HIGHEST
    row_count = lax.axis_size("row")
    block_size = root_diag.shape[0]
    col_count = lax.axis_size("col")
    order_total = block_size * col_count
    loc_rows = order_total // row_count
    row_index = lax.axis_index("row")
    col_index = lax.axis_index("col")
    n_child = child_tiles.shape[0]
    tiles_child = child_tiles.shape[1]
    per_group = tiles_child // row_count
    tiles_block = block_size // TILE
    loc_tiles = loc_rows // TILE
    gathered = lax.all_gather(child_factors, "col", axis=1, tiled=True)
    k_loc = gathered.shape[2]
    tiles4 = gathered.reshape(n_child, tiles_child, TILE, k_loc)
    full_diag = lax.all_gather(root_diag, "col", axis=0, tiled=True)
    owner = child_tiles * TILE // block_size % row_count
    position = jnp.arange(tiles_child, dtype=jnp.int32)
    key = owner * tiles_child + position[None, :]
    rank = jnp.sum(key[:, None, :] < key[:, :, None], axis=2).astype(jnp.int32)
    order = jnp.sum(
        jnp.where(rank[:, :, None] == position[None, None, :], position[None, :, None], 0), axis=1
    ).astype(jnp.int32)
    grouped = pick_tiles(tiles4, order)
    own_tiles = col_index * tiles_block + jnp.arange(tiles_block, dtype=jnp.int32)
    pivot_tiles = jnp.arange(NPAN * tiles_block, dtype=jnp.int32)
    wanted = jnp.concatenate([own_tiles, pivot_tiles])
    match = child_tiles[:, :, None] == wanted[None, None, :]
    where_at = jnp.sum(jnp.where(match, position[None, :, None], 0), axis=1).astype(jnp.int32)
    present = jnp.any(match, axis=1)
    col_rows = pick_tiles(tiles4, where_at)
    col_rows = jnp.where(present[:, :, None, None], col_rows, jnp.zeros_like(col_rows))
    n_cols = wanted.shape[0] * TILE
    col_rows = col_rows.reshape(n_child, n_cols, k_loc)
    pivot_rows = col_rows[:, tiles_block * TILE :]
    grouped = grouped.reshape(n_child, row_count, per_group * TILE, k_loc)
    main = jnp.einsum("cgnk,cmk->gcnm", grouped, col_rows, preferred_element_type=jnp.float32)
    extra = jnp.einsum("cnk,cmk->cnm", pivot_rows, col_rows, preferred_element_type=jnp.float32)
    extra = jnp.broadcast_to(extra[None], (row_count,) + extra.shape)
    packed = jnp.concatenate([main, extra], axis=2)
    chunk_rows = packed.shape[2]
    reduced = lax.psum_scatter(
        packed.reshape(row_count * n_child * chunk_rows, n_cols),
        "row",
        scatter_dimension=0,
        tiled=True,
    ).reshape(n_child, chunk_rows, n_cols)
    mine = reduced[:, : per_group * TILE]
    pivot_part = jnp.sum(reduced[:, per_group * TILE :], axis=0)
    own_w = tiles_block * TILE
    lead_rows = NPAN * block_size
    pivot_diag = full_diag[:lead_rows]
    front00 = pivot_part[:, own_w:] + jnp.diag(pivot_diag)
    lead = jnp.tril(jnp.linalg.cholesky(front00))
    inv_t = lax.linalg.triangular_solve(
        lead, jnp.eye(lead_rows, dtype=jnp.float32), left_side=False, lower=True, transpose_a=True
    )
    cols_panel = jnp.where(col_index == 0, front00, pivot_part[:, :own_w]).T
    my_tiles = lax.dynamic_slice_in_dim(order, row_index * per_group, per_group, axis=1)
    my_root = jnp.take_along_axis(child_tiles, my_tiles, axis=1)
    my_local = my_root * TILE // block_size // row_count * tiles_block + my_root % tiles_block
    loc_index = jnp.arange(loc_tiles, dtype=jnp.int32)
    hit = my_local[:, None, :] == loc_index[None, :, None]
    src = jnp.sum(jnp.where(hit, jnp.arange(per_group, dtype=jnp.int32)[None, None, :], 0), axis=2)
    got = jnp.any(hit, axis=2)
    mine4 = mine.reshape(n_child, per_group, TILE, n_cols)
    placed = pick_tiles(mine4, src.astype(jnp.int32))
    placed = jnp.where(got[:, :, None, None], placed, jnp.zeros_like(placed))
    front_loc = jnp.sum(placed, axis=0).reshape(loc_rows, n_cols)
    local_rows = jnp.arange(loc_rows, dtype=jnp.int32)
    row_block = row_index + local_rows // block_size * row_count
    glob_rows = row_block * block_size + local_rows % block_size
    glob_cols = col_index * block_size + jnp.arange(block_size, dtype=jnp.int32)
    diag_own = jnp.where(glob_rows[:, None] == glob_cols[None, :], root_diag[None, :], 0.0)
    diag_pivot = jnp.where(
        glob_rows[:, None] == jnp.arange(lead_rows, dtype=jnp.int32)[None, :],
        pivot_diag[None, :],
        0.0,
    )
    front_own = front_loc[:, :own_w] + diag_own
    front_pivot = front_loc[:, own_w:] + diag_pivot
    below_rows = jnp.dot(front_pivot, inv_t, precision=highest)
    below_cols = jnp.dot(cols_panel, inv_t, precision=highest)
    schur = front_own - jnp.dot(below_rows, below_cols.T, precision=highest)
    in_lead = (row_block < NPAN)[:, None]
    lead_tiled = jnp.tile(lead, (loc_rows // lead_rows, 1))
    first_col = jnp.where(in_lead, lead_tiled, below_rows)
    rest = jnp.where(in_lead, 0.0, schur)
    return jnp.where(col_index < NPAN, first_col, rest)


def solution(mesh):
    placed = (P(None, "col", "row"), P(), P("col"))
    return jax.shard_map(
        shards, mesh=mesh, in_specs=placed, out_specs=P("row", "col"), check_vma=False
    )
```

profile of v0, /device:TPU:1, one launch (start us, length us, event | category | flops | bytes accessed | tf_op | source)
XLA Modules:
  0.0 355.4 jit_solution(1006790094316008561)
XLA Ops:
  6.5 0.7 all-gather.3.cloned.1.call-update
  7.4 0.9 fusion.44
  8.4 0.7 fusion.48
  9.5 0.9 compare_reduce_fusion
  10.6 75.4 %all-gather.3.cloned.1.call-done = bf16[2,2048,2048]{2,1,0:T(8,128)(2,1)} async-done(((bf16[2,64,2048]{2,1,0:T(8,128)(2,1)}), bf16[2,2048,2048]{2,1,0:T(8,128)(2,1)}) %all-gather.3.cloned.1.call-update) | async-done | bytes 16777232 | tf_op jit(solution)/shard_map/all_gather | solution.py:28
  86.0 8.6 %gather_fusion = bf16[8,128,2048]{2,1,0:T(8,128)(2,1)} fusion(bf16[2,16,128,2048]{3,2,1,0:T(8,128)(2,1)} %bitcast.84, s32[8]{0:T(128)S(1)} %reshape.246), kind=kCustom, calls=%fused_computation | custom fusion | bytes 8388672 | tf_op jit(solution)/shard_map/jit(take_along_axis)/gather | solution.py:11
  94.6 13.1 %gather_fusion.1 = bf16[32,128,2048]{2,1,0:T(8,128)(2,1)} fusion(bf16[2,16,128,2048]{3,2,1,0:T(8,128)(2,1)} %bitcast.85, s32[32]{0:T(128)S(1)} %reshape.252), kind=kCustom, calls=%fused_computation.1 | custom fusion | bytes 33554688 | tf_op jit(solution)/shard_map/jit(take_along_axis)/gather | solution.py:11
  107.7 2.6 fusion.5
  110.3 1.9 copy-done.1
  112.2 1.3 fusion.14
  113.5 15.7 %fusion.6 = f32[4,2,512,512]{3,2,0,1:T(8,128)} fusion(bf16[2,4,512,2048]{3,2,1,0:T(8,128)(2,1)} %bitcast.88, pred[2,4,512]{2,1,0:T(4,128)(4,1)S(1)} %broadcast_in_dim.194, bf16[2,512,2048]{2,1,0:T(8,128)(2,1)} %copy-done.1), kind=kOutput, calls=%fused_computation.15 | convolution fusion | flops 8598323200 | bytes 29364224 | tf_op jit(solution)/shard_map/cgnk,cmk->gcnm/dot_general | solution.py:52
  129.8 8.4 %pad_maximum_fusion = f32[4,2,768,512]{3,2,0,1:T(8,128)} fusion(f32[4,2,256,512]{3,2,0,1:T(8,128)S(1)} %broadcast_in_dim.197, f32[4,2,512,512]{3,2,0,1:T(8,128)} %fusion.6), kind=kLoop, calls=%fused_computation.9 | loop fusion | flops 3145728 | bytes 25165824 | tf_op jit(solution)/shard_map/concatenate | solution.py:55
  138.2 10.7 %copy.27 = f32[4,2,768,512]{3,2,1,0:T(8,128)} copy(f32[4,2,768,512]{3,2,0,1:T(8,128)} %pad_maximum_fusion) | data formatting | bytes 25165824 | tf_op jit(solution)/shard_map/concatenate | solution.py:55
  149.5 24.2 %all-gather = f32[32,1,256]{2,1,0:T(1,128)S(1)} all-gather(f32[1,1,256]{2,1,0:T(1,128)S(1)} %bitcast.95), channel_id=1, replica_groups=mesh['row'=4,'col'=32] {'col'}, dimensions={0}, use_global_device_ids=true | all-gather | bytes 33792 | tf_op jit(solution)/shard_map/all_gather | solution.py:31
  173.9 0.7 gather_fusion.2
  177.2 85.2 %reduce-scatter.2.cloned.1.call-done = f32[1536,512]{1,0:T(8,128)} async-done(((f32[6144,512]{1,0:T(8,128)}), f32[1536,512]{1,0:T(8,128)}) %reduce-scatter.2.cloned.1.call-update) | async-done | bytes 3145744 | tf_op jit(solution)/shard_map/reduce_scatter | solution.py:57
  262.4 1.4 slice_reduce_fusion
  264.2 11.7 %cholesky.49 = f32[128,128]{1,0:T(8,128)S(1)} custom-call(f32[128,128]{1,0:T(8,128)S(1)} %cholesky.115), custom_call_target="Cholesky" | custom-call | tf_op jit(solution)/shard_map/jit(cholesky)/cholesky | solution.py:69
  275.9 9.8 %custom-call.14 = f32[1,128,128]{1,2,0:T(8,128)S(1)} custom-call(f32[1,128,128]{2,1,0:T(8,128)S(1)} %get-tuple-element.44), custom_call_target="InvertDiagBlocksLowerTriangular" | custom-call | tf_op jit(solution)/shard_map/jit(cholesky)/cholesky | solution.py:69
  286.2 11.7 %cholesky.103 = f32[128,128]{1,0:T(8,128)S(1)} custom-call(f32[128,128]{1,0:T(8,128)S(1)} %convolution_subtract_fusion.2), custom_call_target="Cholesky" | custom-call | tf_op jit(solution)/shard_map/jit(cholesky)/cholesky | solution.py:69
  298.3 1.8 slice.99
  300.1 0.7 compare_reduce_fusion.1
  302.8 0.7 triangular_solve.45
  303.6 4.3 %while.1 = (s32[]{:T(128)}, f32[256,256]{0,1:T(8,128)S(1)}, s32[2,2]{1,0:T(2,128)S(1)}, f32[2,128,128]{2,1,0:T(8,128)S(1)}, s32[]{:T(128)}) while((s32[]{:T(128)}, f32[256,256]{0,1:T(8,128)S(1)}, s32[2,2]{1,0:T(2,128)S(1)}, f32[2,128,128]{2,1,0:T(8,128)S(1)}, s32[]{:T(128)}) %tuple.28), condition=%wide.while_cond, body=%wide.while_body.sunk | while | flops 2 | bytes 393321 | solution.py:70
  304.2 1.4 dynamic-slice.7
  306.4 1.4 dynamic-slice.7
  308.6 20.5 %custom-call.15 = f32[2,128,128]{1,2,0:T(8,128)S(1)} custom-call(f32[2,128,128]{2,1,0:T(8,128)} %copy-done.10), custom_call_target="InvertDiagBlocksLowerTriangular" | custom-call | tf_op jit(solution)/shard_map/triangular_solve | solution.py:70
  330.3 1.2 fusion.27
  331.8 4.3 %gather_fusion.3 = f32[32,128,512]{2,1,0:T(8,128)} fusion(f32[2,4,128,512]{3,2,1,0:T(8,128)S(1)} %bitcast.81, s32[32]{0:T(128)S(1)} %reshape.264), kind=kCustom, calls=%fused_computation.3 | custom fusion | bytes 16777472 | tf_op jit(solution)/shard_map/jit(take_along_axis)/gather | solution.py:11
  336.5 6.1 %select_reduce_fusion = f32[16,128,512]{2,1,0:T(8,128)S(1)} fusion(f32[2,16,128,512]{3,2,1,0:T(8,128)} %bitcast.83, pred[2,16]{1,0:T(4,128)(4,1)S(1)} %copy-done.9, pred[2,16]{1,0:T(4,128)(4,1)S(1)} %copy-done.8), kind=kLoop, calls=%fused_computation.10 | loop fusion | flops 5242880 | bytes 12582976 | tf_op jit(solution)/shard_map/reduce_sum | solution.py:84
  342.6 2.0 bitcast_select_fusion.1
  344.7 3.9 %fusion.12 = f32[2048,256]{1,0:T(8,128)} fusion(f32[2048,256]{1,0:T(8,128)S(1)} %get-tuple-element.45, f32[2048,256]{1,0:T(8,128)S(1)} %get-tuple-element.46, f32[256,256]{1,0:T(8,128)S(1)} %fusion.21, f32[2048,512]{1,0:T(8,128)S(1)} %bitcast.87, f32[256]{0:T(256)S(1)} %copy-done.6, s32[256]{0:T(256)S(1)} %copy-done.7, s32[2048]{0:T(1024)S(1)} %fusion.40, ...), kind=kOutput, calls=%fused_computation.18 | convolution fusion | flops 1613758464 | bytes 8663041 | tf_op jit(solution)/shard_map/dot_general | solution.py:99
  (88 shorter events, 10.7 us)
Async XLA Ops:
  6.5 79.4 %all-gather.3.cloned.1.call-start = ((), (), s32[]{:S(2)}) async-start(), calls=%async_computation.1 | async-start | bytes 17301504 | tf_op jit(solution)/shard_map/all_gather | solution.py:28
  7.3 255.1 %reduce-scatter.2.cloned.1.call-start = ((), (), s32[]{:S(2)}) async-start(), calls=%async_computation.2 | async-start | bytes 15728640 | tf_op jit(solution)/shard_map/reduce_scatter | solution.py:57
  110.3 1.9 copy-start.1
  148.8 0.7 copy-start.5
  148.8 25.0 %copy-start = (s32[2,16]{1,0:T(2,128)S(1)}, s32[2,16]{1,0:T(2,128)}, u32[]{:S(2)}) copy-start(s32[2,16]{1,0:T(2,128)} %param.4) | copy-start | bytes 388
  173.7 90.4 %copy-start.3 = (f32[1,1,256]{2,1,0:T(1,128)}, f32[1,1,256]{2,1,0:T(1,128)S(1)}, u32[]{:S(2)}) copy-start(f32[1,1,256]{2,1,0:T(1,128)S(1)} %slice.98) | copy-start | bytes 3076
  307.9 0.7 copy-start.10
  329.1 0.7 copy-start.2
  331.8 4.8 %copy-start.8 = (pred[2,16]{1,0:T(4,128)(4,1)S(1)}, pred[2,16]{1,0:T(4,128)(4,1)}, u32[]{:S(2)}) copy-start(pred[2,16]{1,0:T(4,128)(4,1)} %fusion.45) | copy-start | bytes 100
  331.8 4.8 %copy-start.9 = (pred[2,16]{1,0:T(4,128)(4,1)S(1)}, pred[2,16]{1,0:T(4,128)(4,1)}, u32[]{:S(2)}) copy-start(pred[2,16]{1,0:T(4,128)(4,1)} %compare_and_fusion) | copy-start | bytes 100
  336.5 6.1 %copy-start.4 = (f32[1,1,256]{2,1,0:T(1,128)S(1)}, f32[1,1,256]{2,1,0:T(1,128)}, u32[]{:S(2)}) copy-start(f32[1,1,256]{2,1,0:T(1,128)} %copy-done.3) | copy-start | bytes 3076
  342.6 2.1 copy-start.6
  342.6 2.1 copy-start.7
Sparse Core Ops, SparseCore 0:
  9.6 76.2 all-gather.2
  149.0 113.3 reduce-scatter.1
where the time goes:
time: 356 us; the launch traced here: 355 us
  waiting for transfers between devices  161 us (45%)
  other arithmetic  79 us (22%)
  local copies, waits for them, and re-layouts  50.1 us (14%)
  matrix products  25.5 us (7%)
  blocking collectives  24.2 us (7%)
  between operations  15.2 us (4%)
    reduce_scatter x1, waiting for transfers between devices, shards(): lax.psum_scatter(packed.reshape(row_count * n_child * chunk_rows, n_cols)...  85.2 us
    all_gather x1, waiting for transfers between devices, shards(): gathered = lax.all_gather(child_factors, 'col', axis=1, tiled=True)  75.4 us
    another operation x7, other arithmetic, shards(): lead = jnp.tril(jnp.linalg.cholesky(front00))  34.7 us
    gather x6, local copies, waits for them, and re-layouts, pick_tiles(): return jnp.take_along_axis(tiles4, index[:, :, None, None], axis=1)  26.3 us
    all_gather x1, blocking collectives, shards(): full_diag = lax.all_gather(root_diag, 'col', axis=0, tiled=True)  24.2 us
    another operation x3, other arithmetic, shards(): lax.linalg.triangular_solve(lead, jnp.eye(lead_rows, dtype=jnp.float32),...  21.1 us
    dot_general x1, matrix products, shards(): jnp.einsum('cgnk,cmk->gcnm', grouped, col_rows, preferred_element_type=jn...  15.7 us
    concatenate x1, local copies, waits for them, and re-layouts, shards(): packed = jnp.concatenate([main, extra], axis=2)  10.7 us
  transfers between devices with their start and end apart: 2, of which 2 were waited for; matrix products, arithmetic and copies ran while one was open for 2% of the time, Pallas kernels for 0%

commit v1 on v0

--- a/solution.py
+++ b/solution.py
@@ -28,7 +28,9 @@
     gathered = lax.all_gather(child_factors, "col", axis=1, tiled=True)
     k_loc = gathered.shape[2]
     tiles4 = gathered.reshape(n_child, tiles_child, TILE, k_loc)
-    full_diag = lax.all_gather(root_diag, "col", axis=0, tiled=True)
+    full_diag = jnp.concatenate(
+        lax.all_to_all(jnp.stack([root_diag] * lax.axis_size("col")), "col", 0, 0), axis=0
+    )
     owner = child_tiles * TILE // block_size % row_count
     position = jnp.arange(tiles_child, dtype=jnp.int32)
     key = owner * tiles_child + position[None, :]

time: 356 us -> 356 us (level)
  blocking collectives: 24.2 us -> 0 us
  waiting for transfers between devices: 161 us -> 180 us
  starting transfers between devices: 0.04 us -> 5.48 us
    all_gather x1 -> x0, blocking collectives: 24.2 us -> none  [shards(): full_diag = lax.all_gather(root_diag, 'col', axis=0, tiled=True)]
    reduce_scatter x1, waiting for transfers between devices: 85.2 us -> 99.6 us  [shards(): lax.psum_scatter(packed.reshape(row_count * n_child * chunk_rows, n_cols)...]
    all_to_all x0 -> x1, starting transfers between devices: none -> 5.43 us  [shards(): lax.all_to_all(jnp.stack([root_diag] * lax.axis_size('col')), 'col', 0, 0)]
    all_to_all x0 -> x1, waiting for transfers between devices: none -> 3.79 us  [shards(): lax.all_to_all(jnp.stack([root_diag] * lax.axis_size('col')), 'col', 0, 0)]
  transfers between devices with their start and end apart: 2 -> 3, of which waited for: 2 -> 3; matrix products, arithmetic and copies ran while one was open for 2% -> 2% of each run, Pallas kernels for 0% -> 0%
where the time goes in v1:
time: 356 us; the launch traced here: 355 us
  waiting for transfers between devices  180 us (51%)
  other arithmetic  79 us (22%)
  local copies, waits for them, and re-layouts  50.7 us (14%)
  matrix products  25.5 us (7%)
  between operations  15.1 us (4%)
  starting transfers between devices  5.48 us (2%)
    reduce_scatter x1, waiting for transfers between devices, shards(): lax.psum_scatter(packed.reshape(row_count * n_child * chunk_rows, n_cols)...  99.6 us
    all_gather x1, waiting for transfers between devices, shards(): gathered = lax.all_gather(child_factors, 'col', axis=1, tiled=True)  75.4 us
    another operation x7, other arithmetic, shards(): lead = jnp.tril(jnp.linalg.cholesky(front00))  34.7 us
    gather x6, local copies, waits for them, and re-layouts, pick_tiles(): return jnp.take_along_axis(tiles4, index[:, :, None, None], axis=1)  26.3 us
    another operation x3, other arithmetic, shards(): lax.linalg.triangular_solve(lead, jnp.eye(lead_rows, dtype=jnp.float32),...  21.1 us
    dot_general x1, matrix products, shards(): jnp.einsum('cgnk,cmk->gcnm', grouped, col_rows, preferred_element_type=jn...  15.7 us
    concatenate x1, local copies, waits for them, and re-layouts, shards(): packed = jnp.concatenate([main, extra], axis=2)  10.7 us
    concatenate x1, other arithmetic, shards(): packed = jnp.concatenate([main, extra], axis=2)  8.39 us
  transfers between devices with their start and end apart: 3, of which 3 were waited for; matrix products, arithmetic and copies ran while one was open for 2% of the time, Pallas kernels for 0%

profile of v1, /device:TPU:1, one launch (start us, length us, event | category | flops | bytes accessed | tf_op | source)
XLA Modules:
  0.0 355.4 jit_solution(241768801237081870)
XLA Ops:
  6.5 0.7 all-gather.2.cloned.1.call-update
  7.4 0.9 fusion.44
  8.4 0.7 fusion.48
  9.5 0.9 compare_reduce_fusion
  10.6 75.4 %all-gather.2.cloned.1.call-done = bf16[2,2048,2048]{2,1,0:T(8,128)(2,1)} async-done(((bf16[2,64,2048]{2,1,0:T(8,128)(2,1)}), bf16[2,2048,2048]{2,1,0:T(8,128)(2,1)}) %all-gather.2.cloned.1.call-update) | async-done | bytes 16777232 | tf_op jit(solution)/shard_map/all_gather | solution.py:28
  86.0 8.6 %gather_fusion = bf16[8,128,2048]{2,1,0:T(8,128)(2,1)} fusion(bf16[2,16,128,2048]{3,2,1,0:T(8,128)(2,1)} %bitcast.83, s32[8]{0:T(128)S(1)} %reshape.259), kind=kCustom, calls=%fused_computation | custom fusion | bytes 8388672 | tf_op jit(solution)/shard_map/jit(take_along_axis)/gather | solution.py:11
  94.6 13.1 %gather_fusion.1 = bf16[32,128,2048]{2,1,0:T(8,128)(2,1)} fusion(bf16[2,16,128,2048]{3,2,1,0:T(8,128)(2,1)} %bitcast.84, s32[32]{0:T(128)S(1)} %reshape.265), kind=kCustom, calls=%fused_computation.1 | custom fusion | bytes 33554688 | tf_op jit(solution)/shard_map/jit(take_along_axis)/gather | solution.py:11
  107.7 2.6 fusion.5
  110.3 1.9 copy-done.1
  112.2 1.3 fusion.14
  113.5 15.7 %fusion.6 = f32[4,2,512,512]{3,2,0,1:T(8,128)} fusion(bf16[2,4,512,2048]{3,2,1,0:T(8,128)(2,1)} %bitcast.87, pred[2,4,512]{2,1,0:T(4,128)(4,1)S(1)} %broadcast_in_dim.196, bf16[2,512,2048]{2,1,0:T(8,128)(2,1)} %copy-done.1), kind=kOutput, calls=%fused_computation.15 | convolution fusion | flops 8598323200 | bytes 29364224 | tf_op jit(solution)/shard_map/cgnk,cmk->gcnm/dot_general | solution.py:54
  129.8 8.4 %pad_maximum_fusion = f32[4,2,768,512]{3,2,0,1:T(8,128)} fusion(f32[4,2,256,512]{3,2,0,1:T(8,128)S(1)} %broadcast_in_dim.199, f32[4,2,512,512]{3,2,0,1:T(8,128)} %fusion.6), kind=kLoop, calls=%fused_computation.9 | loop fusion | flops 3145728 | bytes 25165824 | tf_op jit(solution)/shard_map/concatenate | solution.py:57
  138.2 10.7 %copy.27 = f32[4,2,768,512]{3,2,1,0:T(8,128)} copy(f32[4,2,768,512]{3,2,0,1:T(8,128)} %pad_maximum_fusion) | data formatting | bytes 25165824 | tf_op jit(solution)/shard_map/concatenate | solution.py:57
  150.1 5.4 %all-to-all-start = ((f32[32,1,256]{2,1,0:T(1,128)}), f32[32,1,256]{2,1,0:T(1,128)S(1)}, u32[]{:S(2)}, u32[]{:S(2)}) async-start(f32[32,1,256]{2,1,0:T(1,128)} %stack.2), calls=%async_computation.1 | async-start | bytes 65536 | tf_op jit(solution)/shard_map/all_to_all | solution.py:32
  159.0 3.8 %all-to-all-done = f32[32,1,256]{2,1,0:T(1,128)S(1)} async-done(((f32[32,1,256]{2,1,0:T(1,128)}), f32[32,1,256]{2,1,0:T(1,128)S(1)}, u32[]{:S(2)}, u32[]{:S(2)}) %all-to-all-start) | async-done | bytes 32800 | tf_op jit(solution)/shard_map/all_to_all | solution.py:32
  162.8 99.6 %reduce-scatter.2.cloned.1.call-done = f32[1536,512]{1,0:T(8,128)} async-done(((f32[6144,512]{1,0:T(8,128)}), f32[1536,512]{1,0:T(8,128)}) %reduce-scatter.2.cloned.1.call-update) | async-done | bytes 3145744 | tf_op jit(solution)/shard_map/reduce_scatter | solution.py:59
  262.5 1.4 slice_reduce_fusion
  264.2 11.7 %cholesky.49 = f32[128,128]{1,0:T(8,128)S(1)} custom-call(f32[128,128]{1,0:T(8,128)S(1)} %cholesky.115), custom_call_target="Cholesky" | custom-call | tf_op jit(solution)/shard_map/jit(cholesky)/cholesky | solution.py:71
  276.0 9.8 %custom-call.14 = f32[1,128,128]{1,2,0:T(8,128)S(1)} custom-call(f32[1,128,128]{2,1,0:T(8,128)S(1)} %get-tuple-element.44), custom_call_target="InvertDiagBlocksLowerTriangular" | custom-call | tf_op jit(solution)/shard_map/jit(cholesky)/cholesky | solution.py:71
  286.3 11.7 %cholesky.103 = f32[128,128]{1,0:T(8,128)S(1)} custom-call(f32[128,128]{1,0:T(8,128)S(1)} %convolution_subtract_fusion.2), custom_call_target="Cholesky" | custom-call | tf_op jit(solution)/shard_map/jit(cholesky)/cholesky | solution.py:71
  298.3 1.8 slice.100
  300.1 0.7 compare_reduce_fusion.1
  302.9 0.7 triangular_solve.45
  303.6 4.3 %while.1 = (s32[]{:T(128)}, f32[256,256]{0,1:T(8,128)S(1)}, s32[2,2]{1,0:T(2,128)S(1)}, f32[2,128,128]{2,1,0:T(8,128)S(1)}, s32[]{:T(128)}) while((s32[]{:T(128)}, f32[256,256]{0,1:T(8,128)S(1)}, s32[2,2]{1,0:T(2,128)S(1)}, f32[2,128,128]{2,1,0:T(8,128)S(1)}, s32[]{:T(128)}) %tuple.28), condition=%wide.while_cond, body=%wide.while_body.sunk | while | flops 2 | bytes 393321 | solution.py:72
  304.2 1.4 dynamic-slice.7
  306.4 1.4 dynamic-slice.7
  308.6 20.5 %custom-call.15 = f32[2,128,128]{1,2,0:T(8,128)S(1)} custom-call(f32[2,128,128]{2,1,0:T(8,128)} %copy-done.10), custom_call_target="InvertDiagBlocksLowerTriangular" | custom-call | tf_op jit(solution)/shard_map/triangular_solve | solution.py:72
  330.4 1.2 fusion.27
  331.8 4.3 %gather_fusion.3 = f32[32,128,512]{2,1,0:T(8,128)} fusion(f32[2,4,128,512]{3,2,1,0:T(8,128)S(1)} %bitcast.80, s32[32]{0:T(128)S(1)} %reshape.277), kind=kCustom, calls=%fused_computation.3 | custom fusion | bytes 16777472 | tf_op jit(solution)/shard_map/jit(take_along_axis)/gather | solution.py:11
  336.6 6.1 %select_reduce_fusion = f32[16,128,512]{2,1,0:T(8,128)S(1)} fusion(f32[2,16,128,512]{3,2,1,0:T(8,128)} %bitcast.82, pred[2,16]{1,0:T(4,128)(4,1)S(1)} %copy-done.9, pred[2,16]{1,0:T(4,128)(4,1)S(1)} %copy-done.8), kind=kLoop, calls=%fused_computation.10 | loop fusion | flops 5242880 | bytes 12582976 | tf_op jit(solution)/shard_map/reduce_sum | solution.py:86
  342.7 2.0 bitcast_select_fusion.1
  344.7 3.9 %fusion.12 = f32[2048,256]{1,0:T(8,128)} fusion(f32[2048,256]{1,0:T(8,128)S(1)} %get-tuple-element.45, f32[2048,256]{1,0:T(8,128)S(1)} %get-tuple-element.46, f32[256,256]{1,0:T(8,128)S(1)} %fusion.21, f32[2048,512]{1,0:T(8,128)S(1)} %bitcast.86, f32[256]{0:T(256)S(1)} %copy-done.6, s32[256]{0:T(256)S(1)} %copy-done.7, s32[2048]{0:T(1024)S(1)} %fusion.40, ...), kind=kOutput, calls=%fused_computation.18 | convolution fusion | flops 1613758464 | bytes 8663041 | tf_op jit(solution)/shard_map/dot_general | solution.py:101
  (90 shorter events, 12.0 us)
Async XLA Ops:
  6.5 79.4 %all-gather.2.cloned.1.call-start = ((), (), s32[]{:S(2)}) async-start(), calls=%async_computation.2 | async-start | bytes 17301504 | tf_op jit(solution)/shard_map/all_gather | solution.py:28
  7.3 255.2 %reduce-scatter.2.cloned.1.call-start = ((), (), s32[]{:S(2)}) async-start(), calls=%async_computation.3 | async-start | bytes 15728640 | tf_op jit(solution)/shard_map/reduce_scatter | solution.py:59
  110.3 1.9 copy-start.1
  148.8 0.7 copy-start.5
  148.8 6.9 %copy-start = (s32[2,16]{1,0:T(2,128)S(1)}, s32[2,16]{1,0:T(2,128)}, u32[]{:S(2)}) copy-start(s32[2,16]{1,0:T(2,128)} %param.4) | copy-start | bytes 388
  150.1 12.7 %all-to-all-start = ((f32[32,1,256]{2,1,0:T(1,128)}), f32[32,1,256]{2,1,0:T(1,128)S(1)}, u32[]{:S(2)}, u32[]{:S(2)}) async-start(f32[32,1,256]{2,1,0:T(1,128)} %stack.2), calls=%async_computation.1 | async-start | bytes 65536 | tf_op jit(solution)/shard_map/all_to_all | solution.py:32
  162.8 101.3 %copy-start.3 = (f32[1,1,256]{2,1,0:T(1,128)}, f32[1,1,256]{2,1,0:T(1,128)S(1)}, u32[]{:S(2)}) copy-start(f32[1,1,256]{2,1,0:T(1,128)S(1)} %slice.99) | copy-start | bytes 3076
  308.0 0.7 copy-start.10
  329.1 0.7 copy-start.2
  331.8 4.8 %copy-start.8 = (pred[2,16]{1,0:T(4,128)(4,1)S(1)}, pred[2,16]{1,0:T(4,128)(4,1)}, u32[]{:S(2)}) copy-start(pred[2,16]{1,0:T(4,128)(4,1)} %fusion.45) | copy-start | bytes 100
  331.8 4.8 %copy-start.9 = (pred[2,16]{1,0:T(4,128)(4,1)S(1)}, pred[2,16]{1,0:T(4,128)(4,1)}, u32[]{:S(2)}) copy-start(pred[2,16]{1,0:T(4,128)(4,1)} %compare_and_fusion) | copy-start | bytes 100
  336.6 6.1 %copy-start.4 = (f32[1,1,256]{2,1,0:T(1,128)S(1)}, f32[1,1,256]{2,1,0:T(1,128)}, u32[]{:S(2)}) copy-start(f32[1,1,256]{2,1,0:T(1,128)} %copy-done.3) | copy-start | bytes 3076
  342.7 2.1 copy-start.6
  342.7 2.1 copy-start.7
Sparse Core Ops, SparseCore 0:
  9.6 76.2 all-gather.1
  149.0 113.4 reduce-scatter.1
